TPU v7x, 512 devices: a whole 4x4x16 slice. The times are simulated.
512 devices in a mesh: template: 16 (over y, x_hi, core), fsdp: 16 (over z), dp: 2 (over x_lo).
Axes of the slice: x: 4 (x_hi: 2, x_lo: 2; x = x_hi * 2 + x_lo), y: 4, z: 16, core: 2. Of those that a mesh axis runs over, the one named last changes fastest.
Arguments:
- hidden: bfloat16 [16, 4096, 8192], P('template', ('fsdp', 'dp')), may hold values from -6 to 6
- target: bfloat16 [16, 4096, 512], P('template', ('fsdp', 'dp')), may hold values from -6 to 6
- weight: bfloat16 [16, 8192, 512], P('template', 'fsdp'), may hold values from -6 to 6
- gain: bfloat16 [16, 8192], P('template', 'fsdp'), may hold values from 0.099609375 to 1.8984375
Outputs:
- merged_weight: float32 [8192, 512], P(('fsdp', 'dp'))
- merged_gain: float32 [8192], P(('fsdp', 'dp'))
All inputs are finite; a program needn't handle non-finite values.
Results may differ from a plain program's by a relative error of at most 0.0018.
Values may be sent and summed in bfloat16 or wider, within the bound.
No kernel may reach another device: no remote copies, remote signals or barrier semaphores. Data moves between devices by JAX's collectives and lax.ppermute only.
A program may use at most 64 MiB of HBM per device.

v0:
```python
import math
import jax
import jax.numpy as jnp
from jax import lax
from jax.sharding import PartitionSpec as P


def body(hidden, target, weight, gain):
    token_batch = hidden[0]
    goal = target[0]
    w_shard = weight[0]
    g_shard = gain[0]
    width = token_batch.shape[1]
    rows = w_shard.shape[0]
    heads = w_shard.shape[1]
    scale = 1.0 / math.sqrt(width)
    n_t = lax.axis_size("template")
    n_dp = lax.axis_size("dp")
    hidden_f = token_batch.astype(jnp.float32)
    ratio = lax.rsqrt(jnp.mean(jnp.square(hidden_f), axis=1, keepdims=True) + 1e-05)
    swap = [(i, (i + 1) % n_dp) for i in range(n_dp)]
    other_hidden = lax.ppermute(token_batch, "dp", swap)
    other_f = other_hidden.astype(jnp.float32)
    other_ratio = lax.rsqrt(jnp.mean(jnp.square(other_f), axis=1, keepdims=True) + 1e-05)
    half = heads // n_dp
    dp_at = lax.axis_index("dp")
    w_cols = lax.dynamic_slice_in_dim(w_shard, dp_at * half, half, 1)
    w_ext = jnp.concatenate([w_cols, g_shard.reshape(-1, half)], axis=0)
    gathered = lax.all_gather(w_ext, "fsdp", axis=0, tiled=False)
    w_half = gathered[:, :rows, :]
    g_full = gathered[:, rows:, :].reshape(-1).astype(jnp.float32)
    xhat = hidden_f * ratio
    normed = (xhat * g_full[None, :]).astype(jnp.bfloat16)
    other_normed = (other_f * other_ratio * g_full[None, :]).astype(jnp.bfloat16)
    n_blocks = gathered.shape[0]
    mine_half = jnp.einsum(
        "tfr,frh->th",
        normed.reshape(-1, n_blocks, rows),
        w_half,
        preferred_element_type=jnp.float32,
    )
    theirs_half = jnp.einsum(
        "tfr,frh->th",
        other_normed.reshape(-1, n_blocks, rows),
        w_half,
        preferred_element_type=jnp.float32,
    )
    from_other = lax.ppermute(theirs_half, "dp", swap)
    both = jnp.stack([mine_half, from_other])
    first = jnp.where(dp_at == 0, both[0], both[1])
    second = jnp.where(dp_at == 0, both[1], both[0])
    values = jnp.concatenate([first, second], axis=1) * scale
    delta = (values - goal.astype(jnp.float32)).astype(jnp.bfloat16)
    n_f = lax.axis_size("fsdp")
    by_dest = jnp.transpose(token_batch.reshape(token_batch.shape[0], n_f, rows), (1, 0, 2))
    late_batch, _ = lax.optimization_barrier((by_dest, theirs_half))
    local_hidden = lax.all_to_all(late_batch, "fsdp", 0, 0, tiled=True).reshape(-1, rows)
    local_ratio = lax.all_gather(ratio, "fsdp", axis=0, tiled=True)
    local_delta = lax.all_gather(delta, "fsdp", axis=0, tiled=True)
    local_xhat = local_hidden.astype(jnp.float32) * local_ratio
    g_f = g_shard.astype(jnp.float32)
    local_normed = (local_xhat * g_f[None, :]).astype(jnp.bfloat16)
    sq_normed = jnp.square(local_normed.astype(jnp.float32)).astype(jnp.bfloat16)
    sq_delta = jnp.square(local_delta.astype(jnp.float32)).astype(jnp.bfloat16)
    fisher = jnp.einsum("td,th->dh", sq_normed, sq_delta, preferred_element_type=jnp.float32)
    back = jnp.einsum("th,dh->td", local_delta, w_shard, preferred_element_type=jnp.float32) * scale
    gain_info = jnp.sum(jnp.square(back * local_xhat), axis=0)
    extra = jnp.zeros((rows, 128), jnp.float32)
    extra = extra.at[:, 0].set(gain_info * g_f).at[:, 1].set(gain_info)
    pack = jnp.concatenate([fisher * w_shard.astype(jnp.float32), fisher, extra], axis=1)
    cols = pack.shape[1]
    piece = rows // (n_t * n_dp)
    pack = pack.reshape(n_t * n_dp, piece, cols)
    parts = lax.all_to_all(pack, ("dp", "template"), 0, 0, tiled=True)
    total = jnp.sum(parts, axis=0)
    ratio_block = (
        jnp.zeros((piece, 128), jnp.float32)
        .at[:, 0]
        .set(total[:, 2 * heads] / total[:, 2 * heads + 1])
    )
    done = jnp.concatenate([total[:, :heads] / total[:, heads : 2 * heads], ratio_block], axis=1)
    spread = lax.all_to_all(
        jnp.broadcast_to(done[None], (n_t,) + done.shape), "template", 0, 0, tiled=True
    )
    full = spread.reshape(n_t * piece, done.shape[1])
    merged = full[:, :heads]
    merged_gain = full[:, heads]
    return (merged, merged_gain)


def solution(mesh):
    in_specs = (
        P("template", ("fsdp", "dp"), None),
        P("template", ("fsdp", "dp"), None),
        P("template", "fsdp", None),
        P("template", "fsdp"),
    )
    out_specs = (P(("fsdp", "dp"), None), P(("fsdp", "dp")))
    return jax.shard_map(body, mesh=mesh, in_specs=in_specs, out_specs=out_specs, check_vma=False)
```

profile of v0, /device:TPU:1, one launch (start us, length us, event | category | flops | bytes accessed | tf_op | source)
XLA Modules:
  0.0 301.3 jit_solution(15434402891482876748)
XLA Ops:
  7.2 0.0 all-gather.9.cloned.1.call-start
  7.2 0.8 fusion.35
  8.0 1.0 dynamic-slice_bitcast_fusion
  9.0 0.7 maximum_bitcast_fusion
  9.7 0.0 all-gather.9.cloned.1.call-update
  9.7 4.0 %collective-permute-start = (bf16[128,8192]{1,0:T(8,128)(2,1)}, bf16[128,8192]{1,0:T(8,128)(2,1)S(1)}, u32[]{:S(2)}, u32[]{:S(2)}) collective-permute-start(bf16[128,8192]{1,0:T(8,128)(2,1)} %bitcast.50), channel_id=1, source_target_pairs={{0,1},{1,0},{2,3},{3,2},{4,5},{5,4},{6,7},{7,6},{8,9},{9,8},{10,11... | collective-permute-start | bytes 6291464 | tf_op jit(solution)/shard_map/ppermute | solution.py:22
  13.7 2.4 copy.21
  16.1 0.0 copy-start.1
  16.1 1.3 copy-done.1
  17.5 2.5 copy.37
  20.0 34.3 %collective-permute-done = bf16[128,8192]{1,0:T(8,128)(2,1)S(1)} collective-permute-done((bf16[128,8192]{1,0:T(8,128)(2,1)}, bf16[128,8192]{1,0:T(8,128)(2,1)S(1)}, u32[]{:S(2)}, u32[]{:S(2)}) %collective-permute-start) | collective-permute-done | bytes 2097184 | tf_op jit(solution)/shard_map/ppermute | solution.py:22
  54.3 0.5 fusion
  54.8 31.8 %all-gather.9.cloned.1.call-done = bf16[16,514,256]{2,1,0:T(8,128)(2,1)} async-done(((bf16[1,514,256]{2,1,0:T(8,128)(2,1)}), bf16[16,514,256]{2,1,0:T(8,128)(2,1)}) %all-gather.9.cloned.1.call-update) | async-done | bytes 4210704 | tf_op jit(solution)/shard_map/all_gather | solution.py:29
  86.7 1.0 slice_convert_fusion
  87.7 0.6 fusion.2
  88.3 0.6 copy-done.5
  88.9 0.7 fusion.24
  89.6 0.0 copy-start
  89.6 6.2 %all-to-all-start = ((bf16[16,128,512]{2,1,0:T(8,128)(2,1)}), bf16[16,128,512]{2,1,0:T(8,128)(2,1)}, u32[]{:S(2)}, u32[]{:S(2)}) async-start(bf16[16,128,512]{2,1,0:T(8,128)(2,1)} %bitcast.52), calls=%async_computation | async-start | bytes 4194304 | tf_op jit(solution)/shard_map/all_to_all | solution.py:57
  95.9 0.0 all-gather.7.cloned.1.call-start
  95.9 0.5 multiply_reduce_fusion
  96.4 3.1 %collective-permute-start.1 = (f32[128,256]{1,0:T(8,128)S(1)}, f32[128,256]{1,0:T(8,128)S(1)}, u32[]{:S(2)}, u32[]{:S(2)}) collective-permute-start(f32[128,256]{1,0:T(8,128)S(1)} %fusion.24), channel_id=1, source_target_pairs={{0,1},{1,0},{2,3},{3,2},{4,5},{5,4},{6,7},{7,6},{8,9},{9,8},{10,11... | collective-permute-start | bytes 393224 | tf_op jit(solution)/shard_map/ppermute | solution.py:48
  99.6 0.0 copy-start.3
  99.6 0.0 copy-start.2
  99.6 5.5 %fusion.21 = f32[128,256]{1,0:T(8,128)S(1)} fusion(bf16[16,514,256]{2,1,0:T(8,128)(2,1)} %all-gather.9.cloned.1.call-done, f32[16,512]{1,0:T(8,128)S(1)} %bitcast.60, f32[128]{0:T(128)S(1)} %get-tuple-element.49, bf16[128,16,512]{2,1,0:T(8,128)(2,1)} %bitcast.54), kind=kOutput, calls=%fused_computation.29 | convolution fusion | flops 541065216 | bytes 6455808 | tf_op jit(solution)/shard_map/tfr,frh->th/dot_general | solution.py:36
  105.1 0.0 collective-permute-done.1
  105.1 0.0 copy-done.3
  105.1 0.7 fusion.31
  105.8 0.0 all-gather.7.cloned.1.call-update
  105.8 0.2 copy.18
  106.1 0.6 compare_reduce_fusion.1
  106.7 0.6 compare_reduce_fusion
  107.3 111.4 %all-gather.3 = f32[16,1,128]{2,1,0:T(1,128)S(1)} all-gather(f32[1,1,128]{2,1,0:T(1,128)S(1)} %get-tuple-element.48), channel_id=3, replica_groups=mesh['template'=16,'fsdp'=16,'dp'=2] {'fsdp'}, dimensions={0}, use_global_device_ids=true | all-gather | bytes 8704 | tf_op jit(solution)/shard_map/all_gather | solution.py:58
  218.7 2.2 all-gather.7.cloned.1.call-done
  220.9 0.0 all-to-all-done
  220.9 4.0 %fusion.7 = f32[512]{0:T(512)S(1)} fusion(bf16[2048,512]{1,0:T(8,128)(2,1)} %bitcast.16, bf16[2048,512]{1,0:T(8,128)(2,1)} %all-gather.7.cloned.1.call-done, f32[2048]{0:T(1024)S(1)} %bitcast.61, bf16[1,512,512]{2,1,0:T(8,128)(2,1)S(1)} %copy-done.2), kind=kOutput, calls=%fused_computation.10 | convolution fusion | flops 1080032768 | bytes 4728832 | tf_op jit(solution)/shard_map/th,dh->td/dot_general | solution.py:66
  224.9 0.0 copy-done.4
  224.9 1.2 broadcast_select_fusion.2
  226.1 0.2 scatter.11
  226.4 3.3 %convert_multiply_fusion.3 = (f32[512,512]{0,1:T(8,128)S(1)}, f32[512,512]{0,1:T(8,128)S(1)}) fusion(bf16[1,512,512]{1,2,0:T(8,128)(2,1)S(1)} %copy.18, bf16[2048,512]{1,0:T(8,128)(2,1)S(1)} %copy-done.6, bf16[2048,512]{1,0:T(8,128)(2,1)} %bitcast.16, f32[2048]{0:T(1024)S(1)} %bitcast.62, f32[512]{0:T(512)S(1)} %bitcast.63), kind=kOutput, calls=%fused_computation.31 | convolution fusion | flops 1084751872 | bytes 6825984 | tf_op jit(solution)/shard_map/td,th->dh/dot_general | solution.py:65
  229.7 0.2 pad_maximum_fusion
  229.9 2.0 copy.19
  231.9 43.6 %all_to_all.15 = f32[32,16,1152]{2,1,0:T(8,128)S(1)} all-to-all(f32[32,16,1152]{2,1,0:T(8,128)} %bitcast.49), channel_id=1, replica_groups=mesh['template'=16,'fsdp'=16,'dp'=2] {'dp','template'}, dimensions={0} | all-to-all | bytes 4718592 | tf_op jit(solution)/shard_map/all_to_all | solution.py:74
  275.5 0.1 reduce_sum.42
  275.6 0.6 fusion.32
  276.3 16.6 %all_to_all.16 = f32[16,16,640]{2,1,0:T(8,128)S(1)} all-to-all(f32[16,16,640]{2,1,0:T(8,128)S(1)} %broadcast_in_dim.2), channel_id=1, replica_groups=mesh['template'=16,'fsdp'=16,'dp'=2] {'template'}, dimensions={0} | all-to-all | bytes 1310720 | tf_op jit(solution)/shard_map/all_to_all | solution.py:82
  293.0 0.9 slice.81
  293.8 0.7 slice_reduce_fusion
  (16 shorter events, 0.2 us)
Async XLA Ops:
  7.2 79.5 %all-gather.9.cloned.1.call-start = ((), (), s32[]{:S(2)}) async-start(), calls=%async_computation.4 | async-start | bytes 4526080 | tf_op jit(solution)/shard_map/all_gather | solution.py:29
  9.7 44.6 %collective-permute-start = (bf16[128,8192]{1,0:T(8,128)(2,1)}, bf16[128,8192]{1,0:T(8,128)(2,1)S(1)}, u32[]{:S(2)}, u32[]{:S(2)}) collective-permute-start(bf16[128,8192]{1,0:T(8,128)(2,1)} %bitcast.50), channel_id=1, source_target_pairs={{0,1},{1,0},{2,3},{3,2},{4,5},{5,4},{6,7},{7,6},{8,9},{9,8},{10,11... | collective-permute-start | bytes 6291464 | tf_op jit(solution)/shard_map/ppermute | solution.py:22
  16.1 1.4 copy-start.1
  86.7 2.2 copy-start.5
  89.6 6.3 %copy-start = (bf16[1,128,8192]{2,1,0:T(8,128)(2,1)S(1)}, bf16[1,128,8192]{2,1,0:T(8,128)(2,1)}, u32[]{:S(2)}) copy-start(bf16[1,128,8192]{2,1,0:T(8,128)(2,1)} %param.10) | copy-start | bytes 6291460
  89.6 131.3 %all-to-all-start = ((bf16[16,128,512]{2,1,0:T(8,128)(2,1)}), bf16[16,128,512]{2,1,0:T(8,128)(2,1)}, u32[]{:S(2)}, u32[]{:S(2)}) async-start(bf16[16,128,512]{2,1,0:T(8,128)(2,1)} %bitcast.52), calls=%async_computation | async-start | bytes 4194304 | tf_op jit(solution)/shard_map/all_to_all | solution.py:57
  95.9 125.0 %all-gather.7.cloned.1.call-start = ((), (), s32[]{:S(2)}) async-start(), calls=%async_computation.3 | async-start | bytes 2228224 | tf_op jit(solution)/shard_map/all_gather | solution.py:59
  96.4 8.6 %collective-permute-start.1 = (f32[128,256]{1,0:T(8,128)S(1)}, f32[128,256]{1,0:T(8,128)S(1)}, u32[]{:S(2)}, u32[]{:S(2)}) collective-permute-start(f32[128,256]{1,0:T(8,128)S(1)} %fusion.24), channel_id=1, source_target_pairs={{0,1},{1,0},{2,3},{3,2},{4,5},{5,4},{6,7},{7,6},{8,9},{9,8},{10,11... | collective-permute-start | bytes 393224 | tf_op jit(solution)/shard_map/ppermute | solution.py:48
  99.6 5.6 %copy-start.3 = (bf16[1,128,512]{2,1,0:T(8,128)(2,1)S(1)}, bf16[1,128,512]{2,1,0:T(8,128)(2,1)}, u32[]{:S(2)}) copy-start(bf16[1,128,512]{2,1,0:T(8,128)(2,1)} %param.11) | copy-start | bytes 393220
  99.6 6.3 %copy-start.2 = (bf16[1,512,512]{2,1,0:T(8,128)(2,1)S(1)}, bf16[1,512,512]{2,1,0:T(8,128)(2,1)}, u32[]{:S(2)}) copy-start(bf16[1,512,512]{2,1,0:T(8,128)(2,1)} %param.12) | copy-start | bytes 1572868
  220.9 4.0 %copy-start.4 = (bf16[1,512]{1,0:T(2,128)(2,1)S(1)}, bf16[1,512]{1,0:T(2,128)(2,1)}, u32[]{:S(2)}) copy-start(bf16[1,512]{1,0:T(2,128)(2,1)} %param.13) | copy-start | bytes 3076
  220.9 5.5 %copy-start.6 = (bf16[2048,512]{1,0:T(8,128)(2,1)S(1)}, bf16[2048,512]{1,0:T(8,128)(2,1)}, u32[]{:S(2)}) copy-start(bf16[2048,512]{1,0:T(8,128)(2,1)} %all-gather.7.cloned.1.call-done) | copy-start | bytes 6291460
Sparse Core Ops, SparseCore 0:
  10.7 75.9 all-gather.8
  106.0 114.8 all-gather.6
where the time goes:
time: 302 us; the launch traced here: 301 us
  blocking collectives  172 us (57%)
  waiting for transfers between devices  68.4 us (23%)
  between operations  14.3 us (5%)
  matrix products  13.4 us (4%)
  starting transfers between devices  13.3 us (4%)
  local copies, waits for them, and re-layouts  12 us (4%)
  other arithmetic  8.25 us (3%)
    all_gather x1, blocking collectives, body(): local_ratio = lax.all_gather(ratio, 'fsdp', axis=0, tiled=True)  111 us
    all_to_all x1, blocking collectives, body(): parts = lax.all_to_all(pack, ('dp', 'template'), 0, 0, tiled=True)  43.6 us
    ppermute x1, waiting for transfers between devices, body(): other_hidden = lax.ppermute(token_batch, 'dp', swap)  34.3 us
    all_gather x1, waiting for transfers between devices, body(): gathered = lax.all_gather(w_ext, 'fsdp', axis=0, tiled=False)  31.8 us
    all_to_all x1, blocking collectives, body(): lax.all_to_all(jnp.broadcast_to(done[None], (n_t,) + done.shape), 'templa...  16.6 us
    all_to_all x1, starting transfers between devices, body(): lax.all_to_all(late_batch, 'fsdp', 0, 0, tiled=True).reshape(-1, rows)  6.22 us
  transfers between devices with their start and end apart: 5, of which 3 were waited for; matrix products, arithmetic and copies ran while one was open for 5% of the time, Pallas kernels for 0%

commit v1 on v0

--- a/solution.py
+++ b/solution.py
@@ -55,8 +55,11 @@
     by_dest = jnp.transpose(token_batch.reshape(token_batch.shape[0], n_f, rows), (1, 0, 2))
     late_batch, _ = lax.optimization_barrier((by_dest, theirs_half))
     local_hidden = lax.all_to_all(late_batch, "fsdp", 0, 0, tiled=True).reshape(-1, rows)
-    local_ratio = lax.all_gather(ratio, "fsdp", axis=0, tiled=True)
-    local_delta = lax.all_gather(delta, "fsdp", axis=0, tiled=True)
+    local_ratio, local_delta = jnp.split(
+        lax.all_gather(jnp.concatenate([ratio, delta], axis=1), "fsdp", axis=0, tiled=True),
+        [ratio.shape[1]],
+        axis=1,
+    )
     local_xhat = local_hidden.astype(jnp.float32) * local_ratio
     g_f = g_shard.astype(jnp.float32)
     local_normed = (local_xhat * g_f[None, :]).astype(jnp.bfloat16)

time: 302 us -> 339 us (1.12)
  waiting for transfers between devices: 68.4 us -> 214 us
  blocking collectives: 172 us -> 59.1 us
  other arithmetic: 8.25 us -> 12.4 us
    all_gather x1, waiting for transfers between devices: 2.18 us -> 147 us  [body(): lax.all_gather(jnp.concatenate([ratio, delta], axis=1), 'fsdp', axis=0, t...]
    all_gather x1 -> x0, blocking collectives: 111 us -> none  [body(): local_ratio = lax.all_gather(ratio, 'fsdp', axis=0, tiled=True)]
  transfers between devices with their start and end apart: 5 -> 5, of which waited for: 3 -> 3; matrix products, arithmetic and copies ran while one was open for 5% -> 4% of each run, Pallas kernels for 0% -> 0%
where the time goes in v1:
time: 339 us
  waiting for transfers between devices  214 us (63%)
  blocking collectives  59.1 us (17%)
  between operations  14.3 us (4%)
  starting transfers between devices  13.2 us (4%)
  local copies, waits for them, and re-layouts  13 us (4%)
  matrix products  13 us (4%)
  other arithmetic  12.4 us (4%)
    all_gather x1, waiting for transfers between devices, body(): lax.all_gather(jnp.concatenate([ratio, delta], axis=1), 'fsdp', axis=0, t...  147 us
    all_to_all x1, blocking collectives, body(): parts = lax.all_to_all(pack, ('dp', 'template'), 0, 0, tiled=True)  42.5 us
    ppermute x1, waiting for transfers between devices, body(): other_hidden = lax.ppermute(token_batch, 'dp', swap)  36.3 us
    all_gather x1, waiting for transfers between devices, body(): gathered = lax.all_gather(w_ext, 'fsdp', axis=0, tiled=False)  30.1 us
    all_to_all x1, blocking collectives, body(): lax.all_to_all(jnp.broadcast_to(done[None], (n_t,) + done.shape), 'templa...  16.6 us
  transfers between devices with their start and end apart: 5, of which 3 were waited for; matrix products, arithmetic and copies ran while one was open for 4% of the time, Pallas kernels for 0%

profile of v1, /device:TPU:1, one launch (start us, length us, event | category | flops | bytes accessed | tf_op | source)
XLA Modules:
  0.0 338.7 jit_solution(13719820977303705964)
XLA Ops:
  7.2 0.0 copy-start
  7.2 0.0 all-gather.7.cloned.1.call-start
  7.2 0.9 fusion.40
  8.1 1.0 dynamic-slice_bitcast_fusion
  9.1 0.7 maximum_bitcast_fusion
  9.8 0.0 all-gather.7.cloned.1.call-update
  9.8 0.0 all-gather.5.cloned.1.call-start
  9.9 4.0 %collective-permute-start = (bf16[128,8192]{1,0:T(8,128)(2,1)}, bf16[128,8192]{1,0:T(8,128)(2,1)}, u32[]{:S(2)}, u32[]{:S(2)}) collective-permute-start(bf16[128,8192]{1,0:T(8,128)(2,1)} %bitcast.49), channel_id=1, source_target_pairs={{0,1},{1,0},{2,3},{3,2},{4,5},{5,4},{6,7},{7,6},{8,9},{9,8},{10,11... | collective-permute-start | bytes 6291464 | tf_op jit(solution)/shard_map/ppermute | solution.py:22
  13.8 3.7 %copy.24 = bf16[16,8,16,512]{3,2,1,0:T(8,128)(2,1)} copy(bf16[16,8,16,512]{3,1,2,0:T(8,128)(2,1)} %bitcast.50) | data formatting | bytes 4194304
  17.6 0.0 copy-done
  17.6 0.5 multiply_reduce_fusion
  18.1 0.1 copy.20
  18.2 36.3 %collective-permute-done = bf16[128,8192]{1,0:T(8,128)(2,1)} collective-permute-done((bf16[128,8192]{1,0:T(8,128)(2,1)}, bf16[128,8192]{1,0:T(8,128)(2,1)}, u32[]{:S(2)}, u32[]{:S(2)}) %collective-permute-start) | collective-permute-done | bytes 2097184 | tf_op jit(solution)/shard_map/ppermute | solution.py:22
  54.5 2.1 fusion
  56.6 30.1 %all-gather.7.cloned.1.call-done = bf16[16,514,256]{2,1,0:T(8,128)(2,1)} async-done(((bf16[1,514,256]{2,1,0:T(8,128)(2,1)}), bf16[16,514,256]{2,1,0:T(8,128)(2,1)}) %all-gather.7.cloned.1.call-update) | async-done | bytes 4210704 | tf_op jit(solution)/shard_map/all_gather | solution.py:29
  86.7 1.0 slice_convert_fusion
  87.7 2.4 fusion.2
  90.2 0.0 copy-done.5
  90.2 0.7 fusion.28
  90.9 3.1 collective-permute-start.1
  94.1 0.0 copy-start.3
  94.1 2.6 fusion.25
  96.7 0.0 collective-permute-done.1
  96.7 0.0 copy-done.3
  96.8 0.9 pad_maximum_fusion.1
  97.6 0.0 all-gather.5.cloned.1.call-update
  97.7 0.0 copy-start.2
  97.7 2.5 copy.40
  100.2 6.0 %all-to-all-start = ((bf16[16,128,512]{2,1,0:T(8,128)(2,1)}), bf16[16,128,512]{2,1,0:T(8,128)(2,1)S(1)}, u32[]{:S(2)}, u32[]{:S(2)}) async-start(bf16[16,128,512]{2,1,0:T(8,128)(2,1)} %bitcast.53), calls=%async_computation | async-start | bytes 4194304 | tf_op jit(solution)/shard_map/all_to_all | solution.py:57
  106.2 0.2 copy.21
  106.5 0.7 compare_reduce_fusion.1
  107.2 0.6 compare_reduce_fusion
  107.8 147.3 %all-gather.5.cloned.1.call-done = f32[2048,513]{1,0:T(8,128)} async-done(((f32[128,513]{1,0:T(8,128)}), f32[2048,513]{1,0:T(8,128)}) %all-gather.5.cloned.1.call-update) | async-done | bytes 4202512 | tf_op jit(solution)/shard_map/all_gather | solution.py:59
  255.1 1.6 slice_reduce_fusion
  256.6 0.0 copy-start.4
  256.6 0.0 all-to-all-done
  256.6 4.2 %fusion.7 = f32[512]{0:T(512)S(1)} fusion(bf16[16,128,512]{2,1,0:T(8,128)(2,1)S(1)} %all-to-all-done, f32[2048]{0:T(1024)S(1)} %slice_reduce_fusion, f32[2048,513]{1,0:T(8,128)} %all-gather.5.cloned.1.call-done, bf16[1,512,512]{2,1,0:T(8,128)(2,1)S(1)} %copy-done.2), kind=kOutput, calls=%fused_computation.10 | convolution fusion | flops 1080032768 | bytes 4728832 | tf_op jit(solution)/shard_map/th,dh->td/dot_general | solution.py:69
  260.9 1.3 broadcast_select_fusion.2
  262.3 0.2 scatter.11
  262.5 5.5 %convert_multiply_fusion.3 = (f32[512,512]{0,1:T(8,128)S(1)}, f32[512,512]{0,1:T(8,128)S(1)}) fusion(bf16[1,512,512]{1,2,0:T(8,128)(2,1)S(1)} %copy.21, f32[2048,513]{1,0:T(8,128)} %all-gather.5.cloned.1.call-done, bf16[2048,512]{1,0:T(8,128)(2,1)S(1)} %bitcast.56, f32[512]{0:T(512)S(1)} %bitcast.61, f32[2048]{0:T(1024)S(1)} %slice_reduce_fusion), kind=kOutput, calls=%fused_computation.34 | convolution fusion | flops 1083703296 | bytes 8923136 | tf_op jit(solution)/shard_map/td,th->dh/dot_general | solution.py:68
  268.0 0.2 pad_maximum_fusion
  268.2 2.0 copy.22
  270.2 42.5 %all_to_all.15 = f32[32,16,1152]{2,1,0:T(8,128)S(1)} all-to-all(f32[32,16,1152]{2,1,0:T(8,128)} %bitcast.48), channel_id=1, replica_groups=mesh['template'=16,'fsdp'=16,'dp'=2] {'dp','template'}, dimensions={0} | all-to-all | bytes 4718592 | tf_op jit(solution)/shard_map/all_to_all | solution.py:77
  312.7 0.1 reduce_sum.42
  312.9 0.8 fusion.37
  313.7 16.6 %all_to_all.16 = f32[16,16,640]{2,1,0:T(8,128)S(1)} all-to-all(f32[16,16,640]{2,1,0:T(8,128)S(1)} %broadcast_in_dim.2), channel_id=1, replica_groups=mesh['template'=16,'fsdp'=16,'dp'=2] {'template'}, dimensions={0} | all-to-all | bytes 1310720 | tf_op jit(solution)/shard_map/all_to_all | solution.py:85
  330.3 0.9 slice.81
  331.2 0.7 slice_reduce_fusion.1
  (16 shorter events, 0.2 us)
Async XLA Ops:
  7.2 10.4 %copy-start = (bf16[1,128,8192]{2,1,0:T(8,128)(2,1)S(1)}, bf16[1,128,8192]{2,1,0:T(8,128)(2,1)}, u32[]{:S(2)}) copy-start(bf16[1,128,8192]{2,1,0:T(8,128)(2,1)} %param.10) | copy-start | bytes 6291460
  7.2 79.5 %all-gather.7.cloned.1.call-start = ((), (), s32[]{:S(2)}) async-start(), calls=%async_computation.4 | async-start | bytes 4526080 | tf_op jit(solution)/shard_map/all_gather | solution.py:29
  9.8 245.2 %all-gather.5.cloned.1.call-start = ((), (), s32[]{:S(2)}) async-start(), calls=%async_computation.3 | async-start | bytes 5570560 | tf_op jit(solution)/shard_map/all_gather | solution.py:59
  9.9 44.6 %collective-permute-start = (bf16[128,8192]{1,0:T(8,128)(2,1)}, bf16[128,8192]{1,0:T(8,128)(2,1)}, u32[]{:S(2)}, u32[]{:S(2)}) collective-permute-start(bf16[128,8192]{1,0:T(8,128)(2,1)} %bitcast.49), channel_id=1, source_target_pairs={{0,1},{1,0},{2,3},{3,2},{4,5},{5,4},{6,7},{7,6},{8,9},{9,8},{10,11... | collective-permute-start | bytes 6291464 | tf_op jit(solution)/shard_map/ppermute | solution.py:22
  86.7 3.5 %copy-start.5 = (bf16[16,514,256]{2,1,0:T(8,128)(2,1)S(1)}, bf16[16,514,256]{2,1,0:T(8,128)(2,1)}, u32[]{:S(2)}) copy-start(bf16[16,514,256]{2,1,0:T(8,128)(2,1)} %all-gather.7.cloned.1.call-done) | copy-start | bytes 12632068
  90.2 3.9 %copy-start.1 = (bf16[16,8,16,512]{3,2,1,0:T(8,128)(2,1)S(1)}, bf16[16,8,16,512]{3,2,1,0:T(8,128)(2,1)}, u32[]{:S(2)}) copy-start(bf16[16,8,16,512]{3,2,1,0:T(8,128)(2,1)} %copy.24) | copy-start | bytes 6291460
  90.9 5.8 %collective-permute-start.1 = (f32[128,256]{1,0:T(8,128)S(1)}, f32[128,256]{1,0:T(8,128)S(1)}, u32[]{:S(2)}, u32[]{:S(2)}) collective-permute-start(f32[128,256]{1,0:T(8,128)S(1)} %fusion.28), channel_id=1, source_target_pairs={{0,1},{1,0},{2,3},{3,2},{4,5},{5,4},{6,7},{7,6},{8,9},{9,8},{10,11... | collective-permute-start | bytes 393224 | tf_op jit(solution)/shard_map/ppermute | solution.py:48
  94.1 2.7 copy-start.3
  97.7 8.6 %copy-start.2 = (bf16[1,512,512]{2,1,0:T(8,128)(2,1)S(1)}, bf16[1,512,512]{2,1,0:T(8,128)(2,1)}, u32[]{:S(2)}) copy-start(bf16[1,512,512]{2,1,0:T(8,128)(2,1)} %param.12) | copy-start | bytes 1572868
  100.2 156.4 %all-to-all-start = ((bf16[16,128,512]{2,1,0:T(8,128)(2,1)}), bf16[16,128,512]{2,1,0:T(8,128)(2,1)S(1)}, u32[]{:S(2)}, u32[]{:S(2)}) async-start(bf16[16,128,512]{2,1,0:T(8,128)(2,1)} %bitcast.53), calls=%async_computation | async-start | bytes 4194304 | tf_op jit(solution)/shard_map/all_to_all | solution.py:57
  256.6 4.3 %copy-start.4 = (bf16[1,512]{1,0:T(2,128)(2,1)S(1)}, bf16[1,512]{1,0:T(2,128)(2,1)}, u32[]{:S(2)}) copy-start(bf16[1,512]{1,0:T(2,128)(2,1)} %param.13) | copy-start | bytes 3076
Sparse Core Ops, SparseCore 0:
  10.7 75.9 all-gather.6
  97.8 157.2 all-gather.4
